TPU v7x, 32 devices: a whole 2x2x4 slice. The times are simulated.
32 devices in a mesh: section: 2 (over x), fsdp: 16 (over z, y, core).
Axes of the slice: x: 2, y: 2, z: 4, core: 2. Of those that a mesh axis runs over, the one named last changes fastest.
Arguments:
- history: bfloat16 [4, 16, 32, 2048], P(None, 'fsdp'), may hold values from -6 to 6
- keymask: int32 [4, 16, 32], P(None, 'fsdp'), may hold values from 0 to 1, as said below
- codes: int32 [4, 16, 16, 2], P(None, 'fsdp'), may hold values from 0 to 15
- plan_table: bfloat16 [16, 2048], replicated, may hold values from -6 to 6
- query_weights: bfloat16 [2, 2048, 1024], P('section', 'fsdp'), may hold values from -0.125 to 0.125
- output_weights: bfloat16 [2, 1024, 2048], P('section', 'fsdp'), may hold values from -0.75 to 0.75
- gains: float32 [2, 2048], P('section'), may hold values from 0.5 to 1.5
- cotangent: bfloat16 [4, 16, 32, 2048], P(None, 'fsdp'), may hold values from -6 to 6
Outputs:
- section_grads: bfloat16 [2, 4, 16, 32, 2048], P('section', None, 'fsdp')
- gain_grads: float32 [2, 2048], P('section')
Inputs may be any that keep to these rules, and one draw needn't show every extreme that they name: `keymask`: in each series the ones form one run that ends at the last position and covers at least a quarter of the 32 positions.
All inputs are finite; a program needn't handle non-finite values.
Results may differ from a plain program's by a relative error of at most 0.014.
Values may be sent and summed in bfloat16 or wider, within the bound.
No kernel may reach another device: no remote copies, remote signals or barrier semaphores. Data moves between devices by JAX's collectives and lax.ppermute only.
A program may use at most 64 MiB of HBM per device.

v0:
```python
import math
import jax
import jax.numpy as jnp
from jax import lax
from jax.sharding import PartitionSpec as P

HEADS = 8
EPSILON = 1e-05


def shifted(array, axis, by):
    size = lax.axis_size(axis)
    pairs = [(i, i + by) for i in range(size) if 0 <= i + by < size]
    return lax.ppermute(array, axis, pairs)


def rms_scale(inputs, gain_vector):
    return (
        inputs
        * lax.rsqrt(jnp.mean(inputs * inputs, axis=-1, keepdims=True) + EPSILON)
        * gain_vector
    )


def attend_layer(section_input, source, key_mask, query_weight, output_weight, gain_vector):
    series_count, seq_length, model_width = section_input.shape
    half_width = model_width // 2
    head_dim = half_width // HEADS
    head_shape = (series_count, seq_length, HEADS, head_dim)
    input_wide = section_input.astype(jnp.float32)
    normed = rms_scale(input_wide, gain_vector)
    normed_source = rms_scale(source.astype(jnp.float32), gain_vector)
    normed_rows = normed.astype(jnp.bfloat16).reshape(series_count * seq_length, model_width)
    query_flat = jnp.dot(normed_rows, query_weight, preferred_element_type=jnp.float32)
    queries = query_flat.astype(jnp.bfloat16).reshape(head_shape)
    key_rows = normed_source[..., :half_width].astype(jnp.bfloat16).reshape(head_shape)
    value_rows = normed_source[..., half_width:].astype(jnp.bfloat16).reshape(head_shape)
    scores = jnp.einsum(
        "bqhd,bkhd->bhqk", queries, key_rows, preferred_element_type=jnp.float32
    ) / math.sqrt(head_dim)
    raised = jnp.exp(scores) * key_mask.astype(jnp.float32)[:, None, None, :]
    probs = (raised / jnp.sum(raised, axis=-1, keepdims=True)).astype(jnp.bfloat16)
    mixed = jnp.einsum("bhqk,bkhd->bqhd", probs, value_rows, preferred_element_type=jnp.float32)
    mixed = mixed.astype(jnp.bfloat16).reshape(series_count * seq_length, half_width)
    update = jnp.dot(mixed, output_weight, preferred_element_type=jnp.float32)
    return (input_wide + update.reshape(series_count, seq_length, model_width)).astype(jnp.bfloat16)


def pick_slot(stack, slot):
    return lax.dynamic_index_in_dim(stack, slot, 0, False)


def place_slot(stack, slot, update, keep):
    previous = pick_slot(stack, slot)
    return lax.dynamic_update_index_in_dim(stack, jnp.where(keep, update, previous), slot, 0)


def on_device(history, keymask, codes, plan_table, query_weights, output_weights, gains, cotangent):
    section_index = lax.axis_index("section")
    section_count = lax.axis_size("section")
    half_sections = section_count // 2
    micro_count, series_count, seq_length, model_width = history.shape
    gathered_query, gathered_output = (
        lax.all_gather(query_weights, "fsdp", axis=1, tiled=True),
        lax.all_gather(output_weights, "fsdp", axis=1, tiled=True),
    )
    query_weight = gathered_query[0]
    output_weight = gathered_output[0]
    gain_vector = gains[0]
    code_rows = codes.reshape(micro_count, series_count, seq_length)
    code_count = plan_table.shape[0]
    one_hot = (code_rows[..., None] == jnp.arange(code_count, dtype=jnp.int32)).astype(jnp.bfloat16)
    plan_tokens = jnp.einsum(
        "msln,nd->msld", one_hot, plan_table, preferred_element_type=jnp.float32
    ).astype(jnp.bfloat16)
    is_decoder = section_index >= half_sections
    zero_act = jnp.zeros((series_count, seq_length, model_width), jnp.bfloat16)
    zero_stack = jnp.zeros(history.shape, jnp.bfloat16)
    tick_count = micro_count + section_count - 1

    def forward_tick(tick_index, state_tuple):
        got_input, got_memory, inputs_buf, memory_buf = state_tuple
        micro_index = tick_index - section_index
        is_active = (micro_index >= 0) & (micro_index < micro_count)
        slot = jnp.clip(micro_index, 0, micro_count - 1)
        key_mask = pick_slot(keymask, slot)
        section_input = jnp.where(
            section_index == 0,
            pick_slot(history, slot),
            jnp.where(section_index == half_sections, pick_slot(plan_tokens, slot), got_input),
        )
        memory = got_memory
        source = jnp.where(is_decoder, memory, section_input)

        def run_layer():
            return attend_layer(
                section_input, source, key_mask, query_weight, output_weight, gain_vector
            )

        def skip_layer():
            return zero_act

        output = lax.cond(is_active, run_layer, skip_layer)
        inputs_buf = place_slot(inputs_buf, slot, section_input, is_active)
        memory_buf = place_slot(memory_buf, slot, memory, is_active & is_decoder)
        outgoing = jnp.where(
            section_index == half_sections - 1, output, jnp.where(is_decoder, memory, zero_act)
        )
        got_input, got_memory = shifted((output, outgoing), "section", 1)
        return (got_input, got_memory, inputs_buf, memory_buf)

    start_state = (zero_act, zero_act, zero_stack, zero_stack)
    _, _, inputs_buf, memory_buf = lax.fori_loop(0, tick_count, forward_tick, start_state)

    def backward_tick(tick_index, state_tuple):
        got_grad, got_memory_grad, grads_buf, gain_total = state_tuple
        micro_index = tick_index - (section_count - 1 - section_index)
        is_active = (micro_index >= 0) & (micro_index < micro_count)
        slot = jnp.clip(micro_index, 0, micro_count - 1)
        key_mask = pick_slot(keymask, slot)
        out_grad = jnp.where(
            section_index == section_count - 1, pick_slot(cotangent, slot), got_grad
        )
        section_input = pick_slot(inputs_buf, slot)
        memory = pick_slot(memory_buf, slot)

        def section_map(layer_input, layer_memory, layer_gain):
            layer_source = jnp.where(is_decoder, layer_memory, layer_input)
            return attend_layer(
                layer_input, layer_source, key_mask, query_weight, output_weight, layer_gain
            )

        def run_grads():
            _, pull = jax.vjp(section_map, section_input, memory, gain_vector)
            return pull(out_grad)

        def skip_grads():
            return (zero_act, zero_act, jnp.zeros_like(gain_vector))

        input_grad, memory_grad, gain_grad = lax.cond(is_active, run_grads, skip_grads)
        memory_sum = jnp.where(is_decoder, got_memory_grad + memory_grad, zero_act)
        send_main = jnp.where(section_index == half_sections, memory_sum, input_grad)
        send_side = jnp.where(is_decoder & (section_index != half_sections), memory_sum, zero_act)
        got_grad, got_memory_grad = shifted((send_main, send_side), "section", -1)
        grads_buf = place_slot(grads_buf, slot, input_grad, is_active)
        gain_total = gain_total + lax.psum(gain_grad, "fsdp")
        return (got_grad, got_memory_grad, grads_buf, gain_total)

    back_state = (zero_act, zero_act, zero_stack, jnp.zeros_like(gain_vector))
    _, _, grads_buf, gain_total = lax.fori_loop(0, tick_count, backward_tick, back_state)
    return (grads_buf[None], gain_total[None])


def solution(mesh):
    return jax.shard_map(
        on_device,
        mesh=mesh,
        in_specs=(
            P(None, "fsdp", None, None),
            P(None, "fsdp", None),
            P(None, "fsdp", None, None),
            P(),
            P("section", "fsdp", None),
            P("section", "fsdp", None),
            P("section", None),
            P(None, "fsdp", None, None),
        ),
        out_specs=(P("section", None, "fsdp", None, None), P("section", None)),
        check_vma=False,
    )
```

profile of v0, /device:TPU:0, one launch (start us, length us, event | category | flops | bytes accessed | tf_op | source)
XLA Modules:
  0.0 415.8 jit_solution(3246150808287306456)
XLA Ops:
  9.9 53.6 %all-gather.3.cloned.1.call-done = bf16[1,1024,2048]{2,1,0:T(8,128)(2,1)} async-done(((bf16[1,64,2048]{2,1,0:T(8,128)(2,1)}), bf16[1,1024,2048]{2,1,0:T(8,128)(2,1)}) %all-gather.3.cloned.1.call-update) | async-done | bytes 4194320 | tf_op jit(solution)/shard_map/all_gather | solution.py:65
  63.5 51.2 %all-gather.5.cloned.1.call-done = bf16[1,2048,1024]{2,1,0:T(8,128)(2,1)} async-done(((bf16[1,128,1024]{2,1,0:T(8,128)(2,1)}), bf16[1,2048,1024]{2,1,0:T(8,128)(2,1)}) %all-gather.5.cloned.1.call-update) | async-done | bytes 4194320 | tf_op jit(solution)/shard_map/all_gather | solution.py:64
  114.9 89.8 %while.42 = (s32[]{:T(128)}, bf16[1,32,2048]{2,1,0:T(8,128)(2,1)S(1)}, bf16[1,32,2048]{2,1,0:T(8,128)(2,1)S(1)}, bf16[4,1,32,2048]{3,2,1,0:T(8,128)(2,1)S(1)}, b...) while((s32[]{:T(128)}, ...), condition=%wide.region_6.7_spmd, body=%wide.region_0.6_spmd.sunk | while | flops 274366848 | bytes 14173985 | solution.py:113
  116.0 8.3 %conditional.5 = (bf16[1,32,2048]{2,1,0:T(8,128)(2,1)S(1)}) conditional(s32[]{:T(128)} %convert_element_type.398, () %tuple.120, (bf16[1,32,2048]{2,1,0:T(8,128)(2,1)S(1)}, pred[1,32,2048]{2,1,0:T(8,128)(4,1)S(1)}, bf16[1,32,2048]{2,1,0:T(8,128)(2,1)S(1)}, f32[1,2048]{1,0:T(1,128)}, bf16[2048,1024]{1,0:T(8,128)(2,1)}, ...), branch_computations={%region_1.1_spmd, %region_2.5_spmd} | conditional | flops 273973632 | bytes 10700172 | solution.py:103
  117.0 3.1 fusion.5
  121.2 3.0 fusion.1
  124.3 1.3 collective-permute-start
  125.6 1.3 collective-permute-start.1
  127.0 4.8 %collective-permute-done.1 = bf16[1,32,2048]{2,1,0:T(8,128)(2,1)S(1)} collective-permute-done((bf16[1,32,2048]{2,1,0:T(8,128)(2,1)S(1)}, bf16[1,32,2048]{2,1,0:T(8,128)(2,1)S(1)}, u32[]{:S(2)}, u32[]{:S(2)}) %collective-permute-start.1) | collective-permute-done | bytes 131104 | tf_op jit(solution)/shard_map/while/body/eval_jaxpr/ppermute | solution.py:14
  132.9 8.3 %conditional.5 = (bf16[1,32,2048]{2,1,0:T(8,128)(2,1)S(1)}) conditional(s32[]{:T(128)} %convert_element_type.398, () %tuple.120, (bf16[1,32,2048]{2,1,0:T(8,128)(2,1)S(1)}, pred[1,32,2048]{2,1,0:T(8,128)(4,1)S(1)}, bf16[1,32,2048]{2,1,0:T(8,128)(2,1)S(1)}, f32[1,2048]{1,0:T(1,128)}, bf16[2048,1024]{1,0:T(8,128)(2,1)}, ...), branch_computations={%region_1.1_spmd, %region_2.5_spmd} | conditional | flops 273973632 | bytes 10700172 | solution.py:103
  134.0 3.1 fusion.5
  138.2 3.0 fusion.1
  141.2 4.4 %collective-permute-start = (bf16[1,32,2048]{2,1,0:T(8,128)(2,1)S(1)}, bf16[1,32,2048]{2,1,0:T(8,128)(2,1)S(1)}, u32[]{:S(2)}, u32[]{:S(2)}) collective-permute-start(bf16[1,32,2048]{2,1,0:T(8,128)(2,1)S(1)} %get-tuple-element.1286), channel_id=1, source_target_pairs={{0,16},{1,17},{2,18},{3,19},{4,20},{5,21},{6,22},{7,23},{8,24},{9,... | collective-permute-start | bytes 393224 | tf_op jit(solution)/shard_map/while/body/eval_jaxpr/ppermute | solution.py:14
  147.0 4.0 collective-permute-done.1
  152.1 8.3 %conditional.5 = (bf16[1,32,2048]{2,1,0:T(8,128)(2,1)S(1)}) conditional(s32[]{:T(128)} %convert_element_type.398, () %tuple.120, (bf16[1,32,2048]{2,1,0:T(8,128)(2,1)S(1)}, pred[1,32,2048]{2,1,0:T(8,128)(4,1)S(1)}, bf16[1,32,2048]{2,1,0:T(8,128)(2,1)S(1)}, f32[1,2048]{1,0:T(1,128)}, bf16[2048,1024]{1,0:T(8,128)(2,1)}, ...), branch_computations={%region_1.1_spmd, %region_2.5_spmd} | conditional | flops 273973632 | bytes 10700172 | solution.py:103
  153.2 3.1 fusion.5
  157.4 3.0 fusion.1
  160.4 4.4 %collective-permute-start = (bf16[1,32,2048]{2,1,0:T(8,128)(2,1)S(1)}, bf16[1,32,2048]{2,1,0:T(8,128)(2,1)S(1)}, u32[]{:S(2)}, u32[]{:S(2)}) collective-permute-start(bf16[1,32,2048]{2,1,0:T(8,128)(2,1)S(1)} %get-tuple-element.1286), channel_id=1, source_target_pairs={{0,16},{1,17},{2,18},{3,19},{4,20},{5,21},{6,22},{7,23},{8,24},{9,... | collective-permute-start | bytes 393224 | tf_op jit(solution)/shard_map/while/body/eval_jaxpr/ppermute | solution.py:14
  166.2 3.2 collective-permute-done.1
  170.5 8.3 %conditional.5 = (bf16[1,32,2048]{2,1,0:T(8,128)(2,1)S(1)}) conditional(s32[]{:T(128)} %convert_element_type.398, () %tuple.120, (bf16[1,32,2048]{2,1,0:T(8,128)(2,1)S(1)}, pred[1,32,2048]{2,1,0:T(8,128)(4,1)S(1)}, bf16[1,32,2048]{2,1,0:T(8,128)(2,1)S(1)}, f32[1,2048]{1,0:T(1,128)}, bf16[2048,1024]{1,0:T(8,128)(2,1)}, ...), branch_computations={%region_1.1_spmd, %region_2.5_spmd} | conditional | flops 273973632 | bytes 10700172 | solution.py:103
  171.5 3.1 fusion.5
  175.7 3.0 fusion.1
  178.8 4.4 %collective-permute-start = (bf16[1,32,2048]{2,1,0:T(8,128)(2,1)S(1)}, bf16[1,32,2048]{2,1,0:T(8,128)(2,1)S(1)}, u32[]{:S(2)}, u32[]{:S(2)}) collective-permute-start(bf16[1,32,2048]{2,1,0:T(8,128)(2,1)S(1)} %get-tuple-element.1286), channel_id=1, source_target_pairs={{0,16},{1,17},{2,18},{3,19},{4,20},{5,21},{6,22},{7,23},{8,24},{9,... | collective-permute-start | bytes 393224 | tf_op jit(solution)/shard_map/while/body/eval_jaxpr/ppermute | solution.py:14
  184.6 2.5 collective-permute-done.1
  188.2 12.6 %collective-permute-start = (bf16[1,32,2048]{2,1,0:T(8,128)(2,1)S(1)}, bf16[1,32,2048]{2,1,0:T(8,128)(2,1)S(1)}, u32[]{:S(2)}, u32[]{:S(2)}) collective-permute-start(bf16[1,32,2048]{2,1,0:T(8,128)(2,1)S(1)} %get-tuple-element.1286), channel_id=1, source_target_pairs={{0,16},{1,17},{2,18},{3,19},{4,20},{5,21},{6,22},{7,23},{8,24},{9,... | collective-permute-start | bytes 393224 | tf_op jit(solution)/shard_map/while/body/eval_jaxpr/ppermute | solution.py:14
  202.2 2.5 collective-permute-done.1
  204.8 203.3 %while.43 = (s32[]{:T(128)}, bf16[1,32,2048]{2,1,0:T(8,128)(2,1)S(1)}, bf16[1,32,2048]{2,1,0:T(8,128)(2,1)S(1)}, bf16[4,1,32,2048]{3,2,1,0:T(8,128)(2,1)S(1)}, f...) while((s32[]{:T(128)}, ...), condition=%wide.region_19.20_spmd.clone, body=%wide.region_7.19_spmd.clone.sunk | while | flops 417616544 | bytes 54182452 | solution.py:150
  207.6 30.0 %psum.15 = f32[2048]{0:T(1024)S(1)} all-reduce(f32[2048]{0:T(1024)S(1)} %get-tuple-element.1162), channel_id=1, replica_groups=mesh['section'=2,'fsdp'=16] {'fsdp'}, use_global_device_ids=true, to_apply=%region_18.18 | all-reduce | flops 2048 | bytes 16384 | tf_op jit(solution)/shard_map/while/body/eval_jaxpr/psum | solution.py:146
  237.8 9.8 %conditional.6 = (bf16[1,32,2048]{2,1,0:T(8,128)(2,1)S(1)}, bf16[1,32,2048]{2,1,0:T(8,128)(2,1)S(1)}, f32[2048]{0:T(1024)S(1)}) conditional(s32[]{:T(128)} %convert_element_type.399, () %tuple.124, (bf16[4,1,32,2048]{3,2,1,0:T(8,128)(2,1)S(1)}, s32[]{:T(128)}, pred[1,32,2048]{2,1,0:T(32,128)(4,1)S(1)}, bf16[1,32,2048]{2,1,0:T(8,128)(2,1)S(1)}, ...), branch_computations={%region_8.8_spmd, %region_9.17_spmd} | conditional | flops 417282720 | bytes 51716228 | solution.py:140
  239.0 3.1 fusion.38
  243.2 1.3 fusion.37
  245.7 1.5 fusion.50
  250.3 30.0 %psum.15 = f32[2048]{0:T(1024)S(1)} all-reduce(f32[2048]{0:T(1024)S(1)} %get-tuple-element.1162), channel_id=1, replica_groups=mesh['section'=2,'fsdp'=16] {'fsdp'}, use_global_device_ids=true, to_apply=%region_18.18 | all-reduce | flops 2048 | bytes 16384 | tf_op jit(solution)/shard_map/while/body/eval_jaxpr/psum | solution.py:146
  280.4 9.8 %conditional.6 = (bf16[1,32,2048]{2,1,0:T(8,128)(2,1)S(1)}, bf16[1,32,2048]{2,1,0:T(8,128)(2,1)S(1)}, f32[2048]{0:T(1024)S(1)}) conditional(s32[]{:T(128)} %convert_element_type.399, () %tuple.124, (bf16[4,1,32,2048]{3,2,1,0:T(8,128)(2,1)S(1)}, s32[]{:T(128)}, pred[1,32,2048]{2,1,0:T(32,128)(4,1)S(1)}, bf16[1,32,2048]{2,1,0:T(8,128)(2,1)S(1)}, ...), branch_computations={%region_8.8_spmd, %region_9.17_spmd} | conditional | flops 417282720 | bytes 51716228 | solution.py:140
  281.6 3.1 fusion.38
  285.8 1.3 fusion.37
  288.4 1.5 fusion.50
  292.9 30.0 %psum.15 = f32[2048]{0:T(1024)S(1)} all-reduce(f32[2048]{0:T(1024)S(1)} %get-tuple-element.1162), channel_id=1, replica_groups=mesh['section'=2,'fsdp'=16] {'fsdp'}, use_global_device_ids=true, to_apply=%region_18.18 | all-reduce | flops 2048 | bytes 16384 | tf_op jit(solution)/shard_map/while/body/eval_jaxpr/psum | solution.py:146
  323.0 9.8 %conditional.6 = (bf16[1,32,2048]{2,1,0:T(8,128)(2,1)S(1)}, bf16[1,32,2048]{2,1,0:T(8,128)(2,1)S(1)}, f32[2048]{0:T(1024)S(1)}) conditional(s32[]{:T(128)} %convert_element_type.399, () %tuple.124, (bf16[4,1,32,2048]{3,2,1,0:T(8,128)(2,1)S(1)}, s32[]{:T(128)}, pred[1,32,2048]{2,1,0:T(32,128)(4,1)S(1)}, bf16[1,32,2048]{2,1,0:T(8,128)(2,1)S(1)}, ...), branch_computations={%region_8.8_spmd, %region_9.17_spmd} | conditional | flops 417282720 | bytes 51716228 | solution.py:140
  324.2 3.1 fusion.38
  328.4 1.3 fusion.37
  331.0 1.5 fusion.50
  335.5 30.0 %psum.15 = f32[2048]{0:T(1024)S(1)} all-reduce(f32[2048]{0:T(1024)S(1)} %get-tuple-element.1162), channel_id=1, replica_groups=mesh['section'=2,'fsdp'=16] {'fsdp'}, use_global_device_ids=true, to_apply=%region_18.18 | all-reduce | flops 2048 | bytes 16384 | tf_op jit(solution)/shard_map/while/body/eval_jaxpr/psum | solution.py:146
  365.6 9.8 %conditional.6 = (bf16[1,32,2048]{2,1,0:T(8,128)(2,1)S(1)}, bf16[1,32,2048]{2,1,0:T(8,128)(2,1)S(1)}, f32[2048]{0:T(1024)S(1)}) conditional(s32[]{:T(128)} %convert_element_type.399, () %tuple.124, (bf16[4,1,32,2048]{3,2,1,0:T(8,128)(2,1)S(1)}, s32[]{:T(128)}, pred[1,32,2048]{2,1,0:T(32,128)(4,1)S(1)}, bf16[1,32,2048]{2,1,0:T(8,128)(2,1)S(1)}, ...), branch_computations={%region_8.8_spmd, %region_9.17_spmd} | conditional | flops 417282720 | bytes 51716228 | solution.py:140
  366.8 3.1 fusion.38
  371.0 1.3 fusion.37
  373.6 1.5 fusion.50
  378.1 30.0 %psum.15 = f32[2048]{0:T(1024)S(1)} all-reduce(f32[2048]{0:T(1024)S(1)} %get-tuple-element.1162), channel_id=1, replica_groups=mesh['section'=2,'fsdp'=16] {'fsdp'}, use_global_device_ids=true, to_apply=%region_18.18 | all-reduce | flops 2048 | bytes 16384 | tf_op jit(solution)/shard_map/while/body/eval_jaxpr/psum | solution.py:146
  (278 shorter events, 51.1 us)
Async XLA Ops:
  7.2 2.4 copy-start
  7.2 56.3 %all-gather.3.cloned.1.call-start = ((), (), s32[]{:S(2)}) async-start(), calls=%async_computation | async-start | bytes 4456448 | tf_op jit(solution)/shard_map/all_gather | solution.py:65
  7.9 106.8 %all-gather.5.cloned.1.call-start = ((), (), s32[]{:S(2)}) async-start(), calls=%async_computation.1 | async-start | bytes 4456448 | tf_op jit(solution)/shard_map/all_gather | solution.py:64
  114.9 89.9 %copy-start.4 = (bf16[4,1,32,2048]{3,2,1,0:T(8,128)(2,1)S(1)}, bf16[4,1,32,2048]{3,2,1,0:T(8,128)(2,1)}, u32[]{:S(2)}) copy-start(bf16[4,1,32,2048]{3,2,1,0:T(8,128)(2,1)} %param.23) | copy-start | bytes 1572868
  124.3 7.6 %collective-permute-start = (bf16[1,32,2048]{2,1,0:T(8,128)(2,1)S(1)}, bf16[1,32,2048]{2,1,0:T(8,128)(2,1)S(1)}, u32[]{:S(2)}, u32[]{:S(2)}) collective-permute-start(bf16[1,32,2048]{2,1,0:T(8,128)(2,1)S(1)} %get-tuple-element.1286), channel_id=1, source_target_pairs={{0,16},{1,17},{2,18},{3,19},{4,20},{5,21},{6,22},{7,23},{8,24},{9,... | collective-permute-start | bytes 393224 | tf_op jit(solution)/shard_map/while/body/eval_jaxpr/ppermute | solution.py:14
  125.6 6.2 %collective-permute-start.1 = (bf16[1,32,2048]{2,1,0:T(8,128)(2,1)S(1)}, bf16[1,32,2048]{2,1,0:T(8,128)(2,1)S(1)}, u32[]{:S(2)}, u32[]{:S(2)}) collective-permute-start(bf16[1,32,2048]{2,1,0:T(8,128)(2,1)S(1)} %select_select_fusion.2), channel_id=1, source_target_pairs={{0,16},{1,17},{2,18},{3,19},{4,20},{5,21},{6,22},{7,23},{8,24},{9,... | collective-permute-start | bytes 393224 | tf_op jit(solution)/shard_map/while/body/eval_jaxpr/ppermute | solution.py:14
  141.2 9.9 %collective-permute-start = (bf16[1,32,2048]{2,1,0:T(8,128)(2,1)S(1)}, bf16[1,32,2048]{2,1,0:T(8,128)(2,1)S(1)}, u32[]{:S(2)}, u32[]{:S(2)}) collective-permute-start(bf16[1,32,2048]{2,1,0:T(8,128)(2,1)S(1)} %get-tuple-element.1286), channel_id=1, source_target_pairs={{0,16},{1,17},{2,18},{3,19},{4,20},{5,21},{6,22},{7,23},{8,24},{9,... | collective-permute-start | bytes 393224 | tf_op jit(solution)/shard_map/while/body/eval_jaxpr/ppermute | solution.py:14
  145.6 5.4 %collective-permute-start.1 = (bf16[1,32,2048]{2,1,0:T(8,128)(2,1)S(1)}, bf16[1,32,2048]{2,1,0:T(8,128)(2,1)S(1)}, u32[]{:S(2)}, u32[]{:S(2)}) collective-permute-start(bf16[1,32,2048]{2,1,0:T(8,128)(2,1)S(1)} %select_select_fusion.2), channel_id=1, source_target_pairs={{0,16},{1,17},{2,18},{3,19},{4,20},{5,21},{6,22},{7,23},{8,24},{9,... | collective-permute-start | bytes 393224 | tf_op jit(solution)/shard_map/while/body/eval_jaxpr/ppermute | solution.py:14
  160.4 9.0 %collective-permute-start = (bf16[1,32,2048]{2,1,0:T(8,128)(2,1)S(1)}, bf16[1,32,2048]{2,1,0:T(8,128)(2,1)S(1)}, u32[]{:S(2)}, u32[]{:S(2)}) collective-permute-start(bf16[1,32,2048]{2,1,0:T(8,128)(2,1)S(1)} %get-tuple-element.1286), channel_id=1, source_target_pairs={{0,16},{1,17},{2,18},{3,19},{4,20},{5,21},{6,22},{7,23},{8,24},{9,... | collective-permute-start | bytes 393224 | tf_op jit(solution)/shard_map/while/body/eval_jaxpr/ppermute | solution.py:14
  164.8 4.5 %collective-permute-start.1 = (bf16[1,32,2048]{2,1,0:T(8,128)(2,1)S(1)}, bf16[1,32,2048]{2,1,0:T(8,128)(2,1)S(1)}, u32[]{:S(2)}, u32[]{:S(2)}) collective-permute-start(bf16[1,32,2048]{2,1,0:T(8,128)(2,1)S(1)} %select_select_fusion.2), channel_id=1, source_target_pairs={{0,16},{1,17},{2,18},{3,19},{4,20},{5,21},{6,22},{7,23},{8,24},{9,... | collective-permute-start | bytes 393224 | tf_op jit(solution)/shard_map/while/body/eval_jaxpr/ppermute | solution.py:14
  178.8 8.3 %collective-permute-start = (bf16[1,32,2048]{2,1,0:T(8,128)(2,1)S(1)}, bf16[1,32,2048]{2,1,0:T(8,128)(2,1)S(1)}, u32[]{:S(2)}, u32[]{:S(2)}) collective-permute-start(bf16[1,32,2048]{2,1,0:T(8,128)(2,1)S(1)} %get-tuple-element.1286), channel_id=1, source_target_pairs={{0,16},{1,17},{2,18},{3,19},{4,20},{5,21},{6,22},{7,23},{8,24},{9,... | collective-permute-start | bytes 393224 | tf_op jit(solution)/shard_map/while/body/eval_jaxpr/ppermute | solution.py:14
  183.2 3.8 collective-permute-start.1
  188.2 16.5 %collective-permute-start = (bf16[1,32,2048]{2,1,0:T(8,128)(2,1)S(1)}, bf16[1,32,2048]{2,1,0:T(8,128)(2,1)S(1)}, u32[]{:S(2)}, u32[]{:S(2)}) collective-permute-start(bf16[1,32,2048]{2,1,0:T(8,128)(2,1)S(1)} %get-tuple-element.1286), channel_id=1, source_target_pairs={{0,16},{1,17},{2,18},{3,19},{4,20},{5,21},{6,22},{7,23},{8,24},{9,... | collective-permute-start | bytes 393224 | tf_op jit(solution)/shard_map/while/body/eval_jaxpr/ppermute | solution.py:14
  200.8 3.8 collective-permute-start.1
  205.0 32.7 %collective-permute-start.2 = (bf16[1,32,2048]{2,1,0:T(8,128)(2,1)S(1)}, bf16[1,32,2048]{2,1,0:T(8,128)(2,1)S(1)}, u32[]{:S(2)}, u32[]{:S(2)}) collective-permute-start(bf16[1,32,2048]{2,1,0:T(8,128)(2,1)S(1)} %get-tuple-element.1160), channel_id=1, source_target_pairs={{16,0},{17,1},{18,2},{19,3},{20,4},{21,5},{22,6},{23,7},{24,8},{25... | collective-permute-start | bytes 393224 | tf_op jit(solution)/shard_map/while/body/eval_jaxpr/ppermute | solution.py:14
  206.3 31.4 %collective-permute-start.3 = (bf16[1,32,2048]{2,1,0:T(8,128)(2,1)S(1)}, bf16[1,32,2048]{2,1,0:T(8,128)(2,1)S(1)}, u32[]{:S(2)}, u32[]{:S(2)}) collective-permute-start(bf16[1,32,2048]{2,1,0:T(8,128)(2,1)S(1)} %get-tuple-element.1161), channel_id=1, source_target_pairs={{16,0},{17,1},{18,2},{19,3},{20,4},{21,5},{22,6},{23,7},{24,8},{25... | collective-permute-start | bytes 393224 | tf_op jit(solution)/shard_map/while/body/eval_jaxpr/ppermute | solution.py:14
  237.8 5.4 %copy-start.2 = (bf16[1024,2048]{1,0:T(8,128)(2,1)S(1)}, bf16[1024,2048]{1,0:T(8,128)(2,1)}, u32[]{:S(2)}) copy-start(bf16[1024,2048]{1,0:T(8,128)(2,1)} %get-tuple-element.750) | copy-start | bytes 12582916 | tf_op jit(solution)/shard_map/while/body/eval_jaxpr/cond
  242.1 3.1 copy-start.3
  242.1 3.6 copy-start.1
  247.6 32.7 %collective-permute-start.2 = (bf16[1,32,2048]{2,1,0:T(8,128)(2,1)S(1)}, bf16[1,32,2048]{2,1,0:T(8,128)(2,1)S(1)}, u32[]{:S(2)}, u32[]{:S(2)}) collective-permute-start(bf16[1,32,2048]{2,1,0:T(8,128)(2,1)S(1)} %get-tuple-element.1160), channel_id=1, source_target_pairs={{16,0},{17,1},{18,2},{19,3},{20,4},{21,5},{22,6},{23,7},{24,8},{25... | collective-permute-start | bytes 393224 | tf_op jit(solution)/shard_map/while/body/eval_jaxpr/ppermute | solution.py:14
  248.9 31.4 %collective-permute-start.3 = (bf16[1,32,2048]{2,1,0:T(8,128)(2,1)S(1)}, bf16[1,32,2048]{2,1,0:T(8,128)(2,1)S(1)}, u32[]{:S(2)}, u32[]{:S(2)}) collective-permute-start(bf16[1,32,2048]{2,1,0:T(8,128)(2,1)S(1)} %get-tuple-element.1161), channel_id=1, source_target_pairs={{16,0},{17,1},{18,2},{19,3},{20,4},{21,5},{22,6},{23,7},{24,8},{25... | collective-permute-start | bytes 393224 | tf_op jit(solution)/shard_map/while/body/eval_jaxpr/ppermute | solution.py:14
  280.4 5.4 %copy-start.2 = (bf16[1024,2048]{1,0:T(8,128)(2,1)S(1)}, bf16[1024,2048]{1,0:T(8,128)(2,1)}, u32[]{:S(2)}) copy-start(bf16[1024,2048]{1,0:T(8,128)(2,1)} %get-tuple-element.750) | copy-start | bytes 12582916 | tf_op jit(solution)/shard_map/while/body/eval_jaxpr/cond
  284.7 3.1 copy-start.3
  284.8 3.6 copy-start.1
  290.2 32.7 %collective-permute-start.2 = (bf16[1,32,2048]{2,1,0:T(8,128)(2,1)S(1)}, bf16[1,32,2048]{2,1,0:T(8,128)(2,1)S(1)}, u32[]{:S(2)}, u32[]{:S(2)}) collective-permute-start(bf16[1,32,2048]{2,1,0:T(8,128)(2,1)S(1)} %get-tuple-element.1160), channel_id=1, source_target_pairs={{16,0},{17,1},{18,2},{19,3},{20,4},{21,5},{22,6},{23,7},{24,8},{25... | collective-permute-start | bytes 393224 | tf_op jit(solution)/shard_map/while/body/eval_jaxpr/ppermute | solution.py:14
  291.5 31.4 %collective-permute-start.3 = (bf16[1,32,2048]{2,1,0:T(8,128)(2,1)S(1)}, bf16[1,32,2048]{2,1,0:T(8,128)(2,1)S(1)}, u32[]{:S(2)}, u32[]{:S(2)}) collective-permute-start(bf16[1,32,2048]{2,1,0:T(8,128)(2,1)S(1)} %get-tuple-element.1161), channel_id=1, source_target_pairs={{16,0},{17,1},{18,2},{19,3},{20,4},{21,5},{22,6},{23,7},{24,8},{25... | collective-permute-start | bytes 393224 | tf_op jit(solution)/shard_map/while/body/eval_jaxpr/ppermute | solution.py:14
  323.0 5.4 %copy-start.2 = (bf16[1024,2048]{1,0:T(8,128)(2,1)S(1)}, bf16[1024,2048]{1,0:T(8,128)(2,1)}, u32[]{:S(2)}) copy-start(bf16[1024,2048]{1,0:T(8,128)(2,1)} %get-tuple-element.750) | copy-start | bytes 12582916 | tf_op jit(solution)/shard_map/while/body/eval_jaxpr/cond
  327.4 3.1 copy-start.3
  327.4 3.6 copy-start.1
  332.8 32.7 %collective-permute-start.2 = (bf16[1,32,2048]{2,1,0:T(8,128)(2,1)S(1)}, bf16[1,32,2048]{2,1,0:T(8,128)(2,1)S(1)}, u32[]{:S(2)}, u32[]{:S(2)}) collective-permute-start(bf16[1,32,2048]{2,1,0:T(8,128)(2,1)S(1)} %get-tuple-element.1160), channel_id=1, source_target_pairs={{16,0},{17,1},{18,2},{19,3},{20,4},{21,5},{22,6},{23,7},{24,8},{25... | collective-permute-start | bytes 393224 | tf_op jit(solution)/shard_map/while/body/eval_jaxpr/ppermute | solution.py:14
  334.1 31.4 %collective-permute-start.3 = (bf16[1,32,2048]{2,1,0:T(8,128)(2,1)S(1)}, bf16[1,32,2048]{2,1,0:T(8,128)(2,1)S(1)}, u32[]{:S(2)}, u32[]{:S(2)}) collective-permute-start(bf16[1,32,2048]{2,1,0:T(8,128)(2,1)S(1)} %get-tuple-element.1161), channel_id=1, source_target_pairs={{16,0},{17,1},{18,2},{19,3},{20,4},{21,5},{22,6},{23,7},{24,8},{25... | collective-permute-start | bytes 393224 | tf_op jit(solution)/shard_map/while/body/eval_jaxpr/ppermute | solution.py:14
  365.6 5.4 %copy-start.2 = (bf16[1024,2048]{1,0:T(8,128)(2,1)S(1)}, bf16[1024,2048]{1,0:T(8,128)(2,1)}, u32[]{:S(2)}) copy-start(bf16[1024,2048]{1,0:T(8,128)(2,1)} %get-tuple-element.750) | copy-start | bytes 12582916 | tf_op jit(solution)/shard_map/while/body/eval_jaxpr/cond
  370.0 3.1 copy-start.3
  370.0 3.6 copy-start.1
  375.4 32.7 %collective-permute-start.2 = (bf16[1,32,2048]{2,1,0:T(8,128)(2,1)S(1)}, bf16[1,32,2048]{2,1,0:T(8,128)(2,1)S(1)}, u32[]{:S(2)}, u32[]{:S(2)}) collective-permute-start(bf16[1,32,2048]{2,1,0:T(8,128)(2,1)S(1)} %get-tuple-element.1160), channel_id=1, source_target_pairs={{16,0},{17,1},{18,2},{19,3},{20,4},{21,5},{22,6},{23,7},{24,8},{25... | collective-permute-start | bytes 393224 | tf_op jit(solution)/shard_map/while/body/eval_jaxpr/ppermute | solution.py:14
  376.7 31.4 %collective-permute-start.3 = (bf16[1,32,2048]{2,1,0:T(8,128)(2,1)S(1)}, bf16[1,32,2048]{2,1,0:T(8,128)(2,1)S(1)}, u32[]{:S(2)}, u32[]{:S(2)}) collective-permute-start(bf16[1,32,2048]{2,1,0:T(8,128)(2,1)S(1)} %get-tuple-element.1161), channel_id=1, source_target_pairs={{16,0},{17,1},{18,2},{19,3},{20,4},{21,5},{22,6},{23,7},{24,8},{25... | collective-permute-start | bytes 393224 | tf_op jit(solution)/shard_map/while/body/eval_jaxpr/ppermute | solution.py:14
  408.2 0.8 copy-start.5
  408.2 0.8 copy-start.6
Sparse Core Ops, SparseCore 0:
  10.2 53.2 all-gather.2
  65.6 49.0 all-gather.4
where the time goes:
time: 417 us; the launch traced here: 416 us
  blocking collectives  150 us (36%)
  waiting for transfers between devices  123 us (29%)
  matrix products  54.3 us (13%)
  starting transfers between devices  46.6 us (11%)
  other arithmetic  22.1 us (5%)
  between operations  14.2 us (3%)
    psum x5, blocking collectives, backward_tick(): gain_total = gain_total + lax.psum(gain_grad, 'fsdp')  150 us
    all_gather x1, waiting for transfers between devices, on_device(): lax.all_gather(output_weights, 'fsdp', axis=1, tiled=True)  53.6 us
    all_gather x1, waiting for transfers between devices, on_device(): lax.all_gather(query_weights, 'fsdp', axis=1, tiled=True)  51.2 us
    ppermute x20, starting transfers between devices, shifted(): return lax.ppermute(array, axis, pairs)  46.5 us
    dot_general x12, matrix products, attend_layer(): jnp.dot(normed_rows, query_weight, preferred_element_type=jnp.float32)  30.8 us
    dot_general x8, matrix products, attend_layer(): update = jnp.dot(mixed, output_weight, preferred_element_type=jnp.float32)  17.4 us
    ppermute x20, waiting for transfers between devices, shifted(): return lax.ppermute(array, axis, pairs)  17 us
  transfers between devices with their start and end apart: 22, of which 7 were waited for; matrix products, arithmetic and copies ran while one was open for 0% of the time, Pallas kernels for 0%

commit v1 on v0

--- a/solution.py
+++ b/solution.py
@@ -1,3 +1,4 @@
+import functools
 import math
 import jax
 import jax.numpy as jnp
@@ -6,6 +7,33 @@
 
 HEADS = 8
 EPSILON = 1e-05
+
+
+def write_digits(message, dim_k):
+    oldest = list(message.shape[1:])
+    oldest[dim_k] *= message.shape[0]
+    return jnp.moveaxis(message, 0, dim_k).reshape(oldest)
+
+
+def time_windows(vec, shard_axis, d0):
+    shares = lax.psum(1, shard_axis)
+    buffer = [(m, (m + 1) % shares) for m in range(shares)]
+    row_list = [(dd, i0) for i0, dd in buffer]
+    current_block, after = ([], [])
+    for k0 in [*range(shares - 1)]:
+        if k0 % 2 == 0:
+            current_block.append(
+                lax.ppermute(current_block[-1] if current_block else vec, shard_axis, buffer)
+            )
+        else:
+            after.append(lax.ppermute(after[-1] if after else vec, shard_axis, row_list))
+    raw_out = jnp.stack([*current_block[::-1], vec, *after], 0)
+    reply = lax.axis_index(shard_axis) - len(current_block)
+    raw_out = raw_out[(jnp.arange(shares) - reply) % shares]
+    return write_digits(raw_out, d0)
+
+
+part_the_unit = functools.partial(time_windows, shard_axis="fsdp", d0=1)
 
 
 def shifted(array, axis, by):
@@ -61,7 +89,7 @@
     half_sections = section_count // 2
     micro_count, series_count, seq_length, model_width = history.shape
     gathered_query, gathered_output = (
-        lax.all_gather(query_weights, "fsdp", axis=1, tiled=True),
+        part_the_unit(query_weights),
         lax.all_gather(output_weights, "fsdp", axis=1, tiled=True),
     )
     query_weight = gathered_query[0]

time: 417 us -> 383 us (0.918)
  waiting for transfers between devices: 123 us -> 58.2 us
  starting transfers between devices: 46.6 us -> 78 us
  other arithmetic: 22.1 us -> 10.2 us
  local copies, waits for them, and re-layouts: 3.25 us -> 14.3 us
    all_gather x1, waiting for transfers between devices: 53.6 us -> 0.01 us  [on_device(): lax.all_gather(output_weights, 'fsdp', axis=1, tiled=True)]
    all_gather x1 -> x0, waiting for transfers between devices: 51.2 us -> none  [on_device(): lax.all_gather(query_weights, 'fsdp', axis=1, tiled=True)]
    ppermute x0 -> x15, waiting for transfers between devices: none -> 45.2 us  [the longest x8 28.4 us: time_windows(): lax.ppermute(current_block[-1] if current_block else vec, shard_axis, buf...]
    ppermute x0 -> x15, starting transfers between devices: none -> 32.8 us  [the longest x7 32.3 us: time_windows(): lax.ppermute(after[-1] if after else vec, shard_axis, row_list)]
    another operation x8, other arithmetic: 6.99 us -> 0.81 us
    unnamed x9 -> x34, local copies, waits for them, and re-layouts: 1.58 us -> 7.65 us
    convert_element_type x8, other arithmetic: 5.91 us -> 0.07 us  [attend_layer(): raised = jnp.exp(scores) * key_mask.astype(jnp.float32)[:, None, None, :]]
    gather x0 -> x1, local copies, waits for them, and re-layouts: none -> 5.01 us  [time_windows(): raw_out = raw_out[(jnp.arange(shares) - reply) % shares]]
  transfers between devices with their start and end apart: 22 -> 36, of which waited for: 7 -> 19; matrix products, arithmetic and copies ran while one was open for 0% -> 3% of each run, Pallas kernels for 0% -> 0%
where the time goes in v1:
time: 383 us; the launch traced here: 382 us
  blocking collectives  150 us (39%)
  starting transfers between devices  78 us (20%)
  waiting for transfers between devices  58.2 us (15%)
  matrix products  54.7 us (14%)
  local copies, waits for them, and re-layouts  14.3 us (4%)
  between operations  14.3 us (4%)
  other arithmetic  10.2 us (3%)
    psum x5, blocking collectives, backward_tick(): gain_total = gain_total + lax.psum(gain_grad, 'fsdp')  150 us
    ppermute x20, starting transfers between devices, shifted(): return lax.ppermute(array, axis, pairs)  45.2 us
    ppermute x7, starting transfers between devices, time_windows(): lax.ppermute(after[-1] if after else vec, shard_axis, row_list)  32.3 us
    dot_general x12, matrix products, attend_layer(): jnp.dot(normed_rows, query_weight, preferred_element_type=jnp.float32)  31.2 us
    ppermute x8, waiting for transfers between devices, time_windows(): lax.ppermute(current_block[-1] if current_block else vec, shard_axis, buf...  28.4 us
    dot_general x8, matrix products, attend_layer(): update = jnp.dot(mixed, output_weight, preferred_element_type=jnp.float32)  17.4 us
    ppermute x7, waiting for transfers between devices, time_windows(): lax.ppermute(after[-1] if after else vec, shard_axis, row_list)  16.8 us
    ppermute x20, waiting for transfers between devices, shifted(): return lax.ppermute(array, axis, pairs)  12.3 us
  transfers between devices with their start and end apart: 36, of which 19 were waited for; matrix products, arithmetic and copies ran while one was open for 3% of the time, Pallas kernels for 0%

profile of v1, /device:TPU:0, one launch (start us, length us, event | category | flops | bytes accessed | tf_op | source)
XLA Modules:
  0.0 382.0 jit_solution(10761594153587413024)
XLA Ops:
  8.4 9.3 %collective-permute-done.4 = bf16[1,128,1024]{2,1,0:T(8,128)(2,1)S(1)} collective-permute-done((bf16[1,128,1024]{2,1,0:T(8,128)(2,1)}, bf16[1,128,1024]{2,1,0:T(8,128)(2,1)S(1)}, u32[]{:S(2)}, u32[]{:S(2)}) %collective-permute-start.4) | collective-permute-done | bytes 262176 | tf_op jit(solution)/shard_map/ppermute | solution.py:26
  17.7 4.4 %collective-permute-start.12 = (bf16[1,128,1024]{2,1,0:T(8,128)(2,1)}, bf16[1,128,1024]{2,1,0:T(8,128)(2,1)S(1)}, u32[]{:S(2)}, u32[]{:S(2)}) collective-permute-start(bf16[1,128,1024]{2,1,0:T(8,128)(2,1)} %param.20), channel_id=1, source_target_pairs={{1,0},{2,1},{3,2},{4,3},{5,4},{6,5},{7,6},{8,7},{9,8},{10,9},{11,1... | collective-permute-start | bytes 786440 | tf_op jit(solution)/shard_map/ppermute | solution.py:29
  22.1 4.3 %collective-permute-done.5 = bf16[1,128,1024]{2,1,0:T(8,128)(2,1)S(1)} collective-permute-done((bf16[1,128,1024]{2,1,0:T(8,128)(2,1)S(1)}, bf16[1,128,1024]{2,1,0:T(8,128)(2,1)S(1)}, u32[]{:S(2)}, u32[]{:S(2)}) %collective-permute-start.5) | collective-permute-done | bytes 262176 | tf_op jit(solution)/shard_map/ppermute | solution.py:26
  27.3 4.6 %collective-permute-start.13 = (bf16[1,128,1024]{2,1,0:T(8,128)(2,1)S(1)}, bf16[1,128,1024]{2,1,0:T(8,128)(2,1)S(1)}, u32[]{:S(2)}, u32[]{:S(2)}) collective-permute-start(bf16[1,128,1024]{2,1,0:T(8,128)(2,1)S(1)} %collective-permute-done.12), channel_id=1, source_target_pairs={{1,0},{2,1},{3,2},{4,3},{5,4},{6,5},{7,6},{8,7},{9,8},{10,9},{11,1... | collective-permute-start | bytes 786440 | tf_op jit(solution)/shard_map/ppermute | solution.py:29
  31.9 4.5 %collective-permute-done.6 = bf16[1,128,1024]{2,1,0:T(8,128)(2,1)S(1)} collective-permute-done((bf16[1,128,1024]{2,1,0:T(8,128)(2,1)S(1)}, bf16[1,128,1024]{2,1,0:T(8,128)(2,1)S(1)}, u32[]{:S(2)}, u32[]{:S(2)}) %collective-permute-start.6) | collective-permute-done | bytes 262176 | tf_op jit(solution)/shard_map/ppermute | solution.py:26
  37.5 4.7 %collective-permute-start.14 = (bf16[1,128,1024]{2,1,0:T(8,128)(2,1)S(1)}, bf16[1,128,1024]{2,1,0:T(8,128)(2,1)S(1)}, u32[]{:S(2)}, u32[]{:S(2)}) collective-permute-start(bf16[1,128,1024]{2,1,0:T(8,128)(2,1)S(1)} %collective-permute-done.13), channel_id=1, source_target_pairs={{1,0},{2,1},{3,2},{4,3},{5,4},{6,5},{7,6},{8,7},{9,8},{10,9},{11,1... | collective-permute-start | bytes 786440 | tf_op jit(solution)/shard_map/ppermute | solution.py:29
  42.2 2.8 collective-permute-done.7
  45.0 5.9 %collective-permute-done.14 = bf16[1,128,1024]{2,1,0:T(8,128)(2,1)S(1)} collective-permute-done((bf16[1,128,1024]{2,1,0:T(8,128)(2,1)S(1)}, bf16[1,128,1024]{2,1,0:T(8,128)(2,1)S(1)}, u32[]{:S(2)}, u32[]{:S(2)}) %collective-permute-start.14) | collective-permute-done | bytes 262176 | tf_op jit(solution)/shard_map/ppermute | solution.py:29
  50.8 4.6 %collective-permute-start.15 = (bf16[1,128,1024]{2,1,0:T(8,128)(2,1)S(1)}, bf16[1,128,1024]{2,1,0:T(8,128)(2,1)S(1)}, u32[]{:S(2)}, u32[]{:S(2)}) collective-permute-start(bf16[1,128,1024]{2,1,0:T(8,128)(2,1)S(1)} %collective-permute-done.14), channel_id=1, source_target_pairs={{1,0},{2,1},{3,2},{4,3},{5,4},{6,5},{7,6},{8,7},{9,8},{10,9},{11,1... | collective-permute-start | bytes 786440 | tf_op jit(solution)/shard_map/ppermute | solution.py:29
  55.4 3.6 collective-permute-done.8
  59.8 4.7 %collective-permute-start.16 = (bf16[1,128,1024]{2,1,0:T(8,128)(2,1)S(1)}, bf16[1,128,1024]{2,1,0:T(8,128)(2,1)S(1)}, u32[]{:S(2)}, u32[]{:S(2)}) collective-permute-start(bf16[1,128,1024]{2,1,0:T(8,128)(2,1)S(1)} %collective-permute-done.15), channel_id=1, source_target_pairs={{1,0},{2,1},{3,2},{4,3},{5,4},{6,5},{7,6},{8,7},{9,8},{10,9},{11,1... | collective-permute-start | bytes 786440 | tf_op jit(solution)/shard_map/ppermute | solution.py:29
  64.4 3.2 collective-permute-done.9
  67.6 5.9 %collective-permute-done.16 = bf16[1,128,1024]{2,1,0:T(8,128)(2,1)S(1)} collective-permute-done((bf16[1,128,1024]{2,1,0:T(8,128)(2,1)S(1)}, bf16[1,128,1024]{2,1,0:T(8,128)(2,1)S(1)}, u32[]{:S(2)}, u32[]{:S(2)}) %collective-permute-start.16) | collective-permute-done | bytes 262176 | tf_op jit(solution)/shard_map/ppermute | solution.py:29
  73.5 4.6 %collective-permute-start.17 = (bf16[1,128,1024]{2,1,0:T(8,128)(2,1)S(1)}, bf16[1,128,1024]{2,1,0:T(8,128)(2,1)}, u32[]{:S(2)}, u32[]{:S(2)}) collective-permute-start(bf16[1,128,1024]{2,1,0:T(8,128)(2,1)S(1)} %collective-permute-done.16), channel_id=1, source_target_pairs={{1,0},{2,1},{3,2},{4,3},{5,4},{6,5},{7,6},{8,7},{9,8},{10,9},{11,1... | collective-permute-start | bytes 786440 | tf_op jit(solution)/shard_map/ppermute | solution.py:29
  82.0 4.7 %collective-permute-start.18 = (bf16[1,128,1024]{2,1,0:T(8,128)(2,1)}, bf16[1,128,1024]{2,1,0:T(8,128)(2,1)S(1)}, u32[]{:S(2)}, u32[]{:S(2)}) collective-permute-start(bf16[1,128,1024]{2,1,0:T(8,128)(2,1)} %collective-permute-done.17), channel_id=1, source_target_pairs={{1,0},{2,1},{3,2},{4,3},{5,4},{6,5},{7,6},{8,7},{9,8},{10,9},{11,1... | collective-permute-start | bytes 786440 | tf_op jit(solution)/shard_map/ppermute | solution.py:29
  93.4 5.0 %gather_fusion = bf16[16,128,1024]{2,1,0:T(8,128)(2,1)} fusion(bf16[16,128,1024]{2,1,0:T(8,128)(2,1)} %bitcast.261, s32[1024]{0:T(1024)S(1)} %pad_clamp_fusion), kind=kCustom, calls=%fused_computation | custom fusion | bytes 8388672 | tf_op jit(solution)/shard_map/gather | solution.py:32
  98.6 78.4 %while.42 = (s32[]{:T(128)}, bf16[1,32,2048]{2,1,0:T(8,128)(2,1)S(1)}, bf16[1,32,2048]{2,1,0:T(8,128)(2,1)S(1)}, bf16[4,1,32,2048]{3,2,1,0:T(8,128)(2,1)S(1)}, b...) while((s32[]{:T(128)}, ...), condition=%wide.region_6.7_spmd, body=%wide.region_0.6_spmd.sunk | while | flops 274366848 | bytes 14173985 | solution.py:141
  99.7 6.9 %conditional.5 = (bf16[1,32,2048]{2,1,0:T(8,128)(2,1)S(1)}) conditional(s32[]{:T(128)} %convert_element_type.398, () %tuple.120, (bf16[1,32,2048]{2,1,0:T(8,128)(2,1)S(1)}, pred[1,32,2048]{2,1,0:T(8,128)(4,1)S(1)}, bf16[1,32,2048]{2,1,0:T(8,128)(2,1)S(1)}, f32[1,2048]{1,0:T(1,128)S(1)}, bf16[2048,1024]{1,0:T(8,128)(2,1)}, ...), branch_computations={%region_1.1_spmd, %region_2.5_spmd} | conditional | flops 273973632 | bytes 10700172 | solution.py:131
  100.1 3.1 fusion.5
  103.6 3.0 fusion.1
  109.4 2.5 collective-permute-done.1
  112.9 6.9 %conditional.5 = (bf16[1,32,2048]{2,1,0:T(8,128)(2,1)S(1)}) conditional(s32[]{:T(128)} %convert_element_type.398, () %tuple.120, (bf16[1,32,2048]{2,1,0:T(8,128)(2,1)S(1)}, pred[1,32,2048]{2,1,0:T(8,128)(4,1)S(1)}, bf16[1,32,2048]{2,1,0:T(8,128)(2,1)S(1)}, f32[1,2048]{1,0:T(1,128)S(1)}, bf16[2048,1024]{1,0:T(8,128)(2,1)}, ...), branch_computations={%region_1.1_spmd, %region_2.5_spmd} | conditional | flops 273973632 | bytes 10700172 | solution.py:131
  113.3 3.1 fusion.5
  116.8 3.0 fusion.1
  119.9 4.4 %collective-permute-start = (bf16[1,32,2048]{2,1,0:T(8,128)(2,1)S(1)}, bf16[1,32,2048]{2,1,0:T(8,128)(2,1)S(1)}, u32[]{:S(2)}, u32[]{:S(2)}) collective-permute-start(bf16[1,32,2048]{2,1,0:T(8,128)(2,1)S(1)} %get-tuple-element.1286), channel_id=1, source_target_pairs={{0,16},{1,17},{2,18},{3,19},{4,20},{5,21},{6,22},{7,23},{8,24},{9,... | collective-permute-start | bytes 393224 | tf_op jit(solution)/shard_map/while/body/eval_jaxpr/ppermute | solution.py:42
  129.2 6.9 %conditional.5 = (bf16[1,32,2048]{2,1,0:T(8,128)(2,1)S(1)}) conditional(s32[]{:T(128)} %convert_element_type.398, () %tuple.120, (bf16[1,32,2048]{2,1,0:T(8,128)(2,1)S(1)}, pred[1,32,2048]{2,1,0:T(8,128)(4,1)S(1)}, bf16[1,32,2048]{2,1,0:T(8,128)(2,1)S(1)}, f32[1,2048]{1,0:T(1,128)S(1)}, bf16[2048,1024]{1,0:T(8,128)(2,1)}, ...), branch_computations={%region_1.1_spmd, %region_2.5_spmd} | conditional | flops 273973632 | bytes 10700172 | solution.py:131
  129.6 3.1 fusion.5
  133.1 3.0 fusion.1
  136.2 4.4 %collective-permute-start = (bf16[1,32,2048]{2,1,0:T(8,128)(2,1)S(1)}, bf16[1,32,2048]{2,1,0:T(8,128)(2,1)S(1)}, u32[]{:S(2)}, u32[]{:S(2)}) collective-permute-start(bf16[1,32,2048]{2,1,0:T(8,128)(2,1)S(1)} %get-tuple-element.1286), channel_id=1, source_target_pairs={{0,16},{1,17},{2,18},{3,19},{4,20},{5,21},{6,22},{7,23},{8,24},{9,... | collective-permute-start | bytes 393224 | tf_op jit(solution)/shard_map/while/body/eval_jaxpr/ppermute | solution.py:42
  145.5 6.9 %conditional.5 = (bf16[1,32,2048]{2,1,0:T(8,128)(2,1)S(1)}) conditional(s32[]{:T(128)} %convert_element_type.398, () %tuple.120, (bf16[1,32,2048]{2,1,0:T(8,128)(2,1)S(1)}, pred[1,32,2048]{2,1,0:T(8,128)(4,1)S(1)}, bf16[1,32,2048]{2,1,0:T(8,128)(2,1)S(1)}, f32[1,2048]{1,0:T(1,128)S(1)}, bf16[2048,1024]{1,0:T(8,128)(2,1)}, ...), branch_computations={%region_1.1_spmd, %region_2.5_spmd} | conditional | flops 273973632 | bytes 10700172 | solution.py:131
  145.9 3.1 fusion.5
  149.4 3.0 fusion.1
  152.5 4.4 %collective-permute-start = (bf16[1,32,2048]{2,1,0:T(8,128)(2,1)S(1)}, bf16[1,32,2048]{2,1,0:T(8,128)(2,1)S(1)}, u32[]{:S(2)}, u32[]{:S(2)}) collective-permute-start(bf16[1,32,2048]{2,1,0:T(8,128)(2,1)S(1)} %get-tuple-element.1286), channel_id=1, source_target_pairs={{0,16},{1,17},{2,18},{3,19},{4,20},{5,21},{6,22},{7,23},{8,24},{9,... | collective-permute-start | bytes 393224 | tf_op jit(solution)/shard_map/while/body/eval_jaxpr/ppermute | solution.py:42
  161.9 11.3 %collective-permute-start = (bf16[1,32,2048]{2,1,0:T(8,128)(2,1)S(1)}, bf16[1,32,2048]{2,1,0:T(8,128)(2,1)S(1)}, u32[]{:S(2)}, u32[]{:S(2)}) collective-permute-start(bf16[1,32,2048]{2,1,0:T(8,128)(2,1)S(1)} %get-tuple-element.1286), channel_id=1, source_target_pairs={{0,16},{1,17},{2,18},{3,19},{4,20},{5,21},{6,22},{7,23},{8,24},{9,... | collective-permute-start | bytes 393224 | tf_op jit(solution)/shard_map/while/body/eval_jaxpr/ppermute | solution.py:42
  177.2 197.1 %while.43 = (s32[]{:T(128)}, bf16[1,32,2048]{2,1,0:T(8,128)(2,1)S(1)}, bf16[1,32,2048]{2,1,0:T(8,128)(2,1)S(1)}, bf16[4,1,32,2048]{3,2,1,0:T(8,128)(2,1)S(1)}, f...) while((s32[]{:T(128)}, ...), condition=%wide.region_19.20_spmd.clone, body=%wide.region_7.19_spmd.clone.sunk | while | flops 417616544 | bytes 54149656 | solution.py:178
  180.0 30.0 %psum.15 = f32[2048]{0:T(1024)S(1)} all-reduce(f32[2048]{0:T(1024)S(1)} %get-tuple-element.1162), channel_id=1, replica_groups=mesh['section'=2,'fsdp'=16] {'fsdp'}, use_global_device_ids=true, to_apply=%region_18.18 | all-reduce | flops 2048 | bytes 16384 | tf_op jit(solution)/shard_map/while/body/eval_jaxpr/psum | solution.py:174
  210.1 8.2 %conditional.6 = (bf16[1,32,2048]{2,1,0:T(8,128)(2,1)S(1)}, bf16[1,32,2048]{2,1,0:T(8,128)(2,1)S(1)}, f32[2048]{0:T(1024)S(1)}) conditional(s32[]{:T(128)} %convert_element_type.399, () %tuple.124, (bf16[4,1,32,2048]{3,2,1,0:T(8,128)(2,1)S(1)}, s32[]{:T(128)}, pred[1,32,2048]{2,1,0:T(32,128)(4,1)S(1)}, bf16[1,32,2048]{2,1,0:T(8,128)(2,1)S(1)}, ...), branch_computations={%region_8.8_spmd, %region_9.17_spmd} | conditional | flops 417282720 | bytes 51683432 | solution.py:168
  210.5 3.3 fusion.38
  221.1 30.0 %psum.15 = f32[2048]{0:T(1024)S(1)} all-reduce(f32[2048]{0:T(1024)S(1)} %get-tuple-element.1162), channel_id=1, replica_groups=mesh['section'=2,'fsdp'=16] {'fsdp'}, use_global_device_ids=true, to_apply=%region_18.18 | all-reduce | flops 2048 | bytes 16384 | tf_op jit(solution)/shard_map/while/body/eval_jaxpr/psum | solution.py:174
  251.2 8.2 %conditional.6 = (bf16[1,32,2048]{2,1,0:T(8,128)(2,1)S(1)}, bf16[1,32,2048]{2,1,0:T(8,128)(2,1)S(1)}, f32[2048]{0:T(1024)S(1)}) conditional(s32[]{:T(128)} %convert_element_type.399, () %tuple.124, (bf16[4,1,32,2048]{3,2,1,0:T(8,128)(2,1)S(1)}, s32[]{:T(128)}, pred[1,32,2048]{2,1,0:T(32,128)(4,1)S(1)}, bf16[1,32,2048]{2,1,0:T(8,128)(2,1)S(1)}, ...), branch_computations={%region_8.8_spmd, %region_9.17_spmd} | conditional | flops 417282720 | bytes 51683432 | solution.py:168
  251.6 3.2 fusion.38
  262.1 30.0 %psum.15 = f32[2048]{0:T(1024)S(1)} all-reduce(f32[2048]{0:T(1024)S(1)} %get-tuple-element.1162), channel_id=1, replica_groups=mesh['section'=2,'fsdp'=16] {'fsdp'}, use_global_device_ids=true, to_apply=%region_18.18 | all-reduce | flops 2048 | bytes 16384 | tf_op jit(solution)/shard_map/while/body/eval_jaxpr/psum | solution.py:174
  292.2 8.2 %conditional.6 = (bf16[1,32,2048]{2,1,0:T(8,128)(2,1)S(1)}, bf16[1,32,2048]{2,1,0:T(8,128)(2,1)S(1)}, f32[2048]{0:T(1024)S(1)}) conditional(s32[]{:T(128)} %convert_element_type.399, () %tuple.124, (bf16[4,1,32,2048]{3,2,1,0:T(8,128)(2,1)S(1)}, s32[]{:T(128)}, pred[1,32,2048]{2,1,0:T(32,128)(4,1)S(1)}, bf16[1,32,2048]{2,1,0:T(8,128)(2,1)S(1)}, ...), branch_computations={%region_8.8_spmd, %region_9.17_spmd} | conditional | flops 417282720 | bytes 51683432 | solution.py:168
  292.6 3.3 fusion.38
  303.2 30.0 %psum.15 = f32[2048]{0:T(1024)S(1)} all-reduce(f32[2048]{0:T(1024)S(1)} %get-tuple-element.1162), channel_id=1, replica_groups=mesh['section'=2,'fsdp'=16] {'fsdp'}, use_global_device_ids=true, to_apply=%region_18.18 | all-reduce | flops 2048 | bytes 16384 | tf_op jit(solution)/shard_map/while/body/eval_jaxpr/psum | solution.py:174
  333.3 8.2 %conditional.6 = (bf16[1,32,2048]{2,1,0:T(8,128)(2,1)S(1)}, bf16[1,32,2048]{2,1,0:T(8,128)(2,1)S(1)}, f32[2048]{0:T(1024)S(1)}) conditional(s32[]{:T(128)} %convert_element_type.399, () %tuple.124, (bf16[4,1,32,2048]{3,2,1,0:T(8,128)(2,1)S(1)}, s32[]{:T(128)}, pred[1,32,2048]{2,1,0:T(32,128)(4,1)S(1)}, bf16[1,32,2048]{2,1,0:T(8,128)(2,1)S(1)}, ...), branch_computations={%region_8.8_spmd, %region_9.17_spmd} | conditional | flops 417282720 | bytes 51683432 | solution.py:168
  333.7 3.3 fusion.38
  344.3 30.0 %psum.15 = f32[2048]{0:T(1024)S(1)} all-reduce(f32[2048]{0:T(1024)S(1)} %get-tuple-element.1162), channel_id=1, replica_groups=mesh['section'=2,'fsdp'=16] {'fsdp'}, use_global_device_ids=true, to_apply=%region_18.18 | all-reduce | flops 2048 | bytes 16384 | tf_op jit(solution)/shard_map/while/body/eval_jaxpr/psum | solution.py:174
  (326 shorter events, 74.6 us)
Async XLA Ops:
  7.2 72.1 %copy-start = (bf16[16,2048]{1,0:T(8,128)(2,1)S(1)}, bf16[16,2048]{1,0:T(8,128)(2,1)}, u32[]{:S(2)}) copy-start(bf16[16,2048]{1,0:T(8,128)(2,1)} %param.19) | copy-start | bytes 196612
  7.2 83.1 %copy-start.7 = (bf16[1,128,1024]{2,1,0:T(8,128)(2,1)S(1)}, bf16[1,128,1024]{2,1,0:T(8,128)(2,1)}, u32[]{:S(2)}) copy-start(bf16[1,128,1024]{2,1,0:T(8,128)(2,1)} %param.20) | copy-start | bytes 786436
  7.2 91.2 %all-gather.2.cloned.1.call-start = ((), (), s32[]{:S(2)}) async-start(), calls=%async_computation | async-start | bytes 4456448 | tf_op jit(solution)/shard_map/all_gather | solution.py:93
  7.9 9.8 %collective-permute-start.4 = (bf16[1,128,1024]{2,1,0:T(8,128)(2,1)}, bf16[1,128,1024]{2,1,0:T(8,128)(2,1)S(1)}, u32[]{:S(2)}, u32[]{:S(2)}) collective-permute-start(bf16[1,128,1024]{2,1,0:T(8,128)(2,1)} %param.20), channel_id=1, source_target_pairs={{0,1},{1,2},{2,3},{3,4},{4,5},{5,6},{6,7},{7,8},{8,9},{9,10},{10,1... | collective-permute-start | bytes 786440 | tf_op jit(solution)/shard_map/ppermute | solution.py:26
  17.7 8.7 %collective-permute-start.5 = (bf16[1,128,1024]{2,1,0:T(8,128)(2,1)S(1)}, bf16[1,128,1024]{2,1,0:T(8,128)(2,1)S(1)}, u32[]{:S(2)}, u32[]{:S(2)}) collective-permute-start(bf16[1,128,1024]{2,1,0:T(8,128)(2,1)S(1)} %collective-permute-done.4), channel_id=1, source_target_pairs={{0,1},{1,2},{2,3},{3,4},{4,5},{5,6},{6,7},{7,8},{8,9},{9,10},{10,1... | collective-permute-start | bytes 786440 | tf_op jit(solution)/shard_map/ppermute | solution.py:26
  17.7 9.6 %collective-permute-start.12 = (bf16[1,128,1024]{2,1,0:T(8,128)(2,1)}, bf16[1,128,1024]{2,1,0:T(8,128)(2,1)S(1)}, u32[]{:S(2)}, u32[]{:S(2)}) collective-permute-start(bf16[1,128,1024]{2,1,0:T(8,128)(2,1)} %param.20), channel_id=1, source_target_pairs={{1,0},{2,1},{3,2},{4,3},{5,4},{6,5},{7,6},{8,7},{9,8},{10,9},{11,1... | collective-permute-start | bytes 786440 | tf_op jit(solution)/shard_map/ppermute | solution.py:29
  26.4 10.0 %collective-permute-start.6 = (bf16[1,128,1024]{2,1,0:T(8,128)(2,1)S(1)}, bf16[1,128,1024]{2,1,0:T(8,128)(2,1)S(1)}, u32[]{:S(2)}, u32[]{:S(2)}) collective-permute-start(bf16[1,128,1024]{2,1,0:T(8,128)(2,1)S(1)} %collective-permute-done.5), channel_id=1, source_target_pairs={{0,1},{1,2},{2,3},{3,4},{4,5},{5,6},{6,7},{7,8},{8,9},{9,10},{10,1... | collective-permute-start | bytes 786440 | tf_op jit(solution)/shard_map/ppermute | solution.py:26
  27.3 10.2 %collective-permute-start.13 = (bf16[1,128,1024]{2,1,0:T(8,128)(2,1)S(1)}, bf16[1,128,1024]{2,1,0:T(8,128)(2,1)S(1)}, u32[]{:S(2)}, u32[]{:S(2)}) collective-permute-start(bf16[1,128,1024]{2,1,0:T(8,128)(2,1)S(1)} %collective-permute-done.12), channel_id=1, source_target_pairs={{1,0},{2,1},{3,2},{4,3},{5,4},{6,5},{7,6},{8,7},{9,8},{10,9},{11,1... | collective-permute-start | bytes 786440 | tf_op jit(solution)/shard_map/ppermute | solution.py:29
  36.4 8.6 %collective-permute-start.7 = (bf16[1,128,1024]{2,1,0:T(8,128)(2,1)S(1)}, bf16[1,128,1024]{2,1,0:T(8,128)(2,1)S(1)}, u32[]{:S(2)}, u32[]{:S(2)}) collective-permute-start(bf16[1,128,1024]{2,1,0:T(8,128)(2,1)S(1)} %collective-permute-done.6), channel_id=1, source_target_pairs={{0,1},{1,2},{2,3},{3,4},{4,5},{5,6},{6,7},{7,8},{8,9},{9,10},{10,1... | collective-permute-start | bytes 786440 | tf_op jit(solution)/shard_map/ppermute | solution.py:26
  37.5 13.3 %collective-permute-start.14 = (bf16[1,128,1024]{2,1,0:T(8,128)(2,1)S(1)}, bf16[1,128,1024]{2,1,0:T(8,128)(2,1)S(1)}, u32[]{:S(2)}, u32[]{:S(2)}) collective-permute-start(bf16[1,128,1024]{2,1,0:T(8,128)(2,1)S(1)} %collective-permute-done.13), channel_id=1, source_target_pairs={{1,0},{2,1},{3,2},{4,3},{5,4},{6,5},{7,6},{8,7},{9,8},{10,9},{11,1... | collective-permute-start | bytes 786440 | tf_op jit(solution)/shard_map/ppermute | solution.py:29
  45.0 14.1 %collective-permute-start.8 = (bf16[1,128,1024]{2,1,0:T(8,128)(2,1)S(1)}, bf16[1,128,1024]{2,1,0:T(8,128)(2,1)S(1)}, u32[]{:S(2)}, u32[]{:S(2)}) collective-permute-start(bf16[1,128,1024]{2,1,0:T(8,128)(2,1)S(1)} %collective-permute-done.7), channel_id=1, source_target_pairs={{0,1},{1,2},{2,3},{3,4},{4,5},{5,6},{6,7},{7,8},{8,9},{9,10},{10,1... | collective-permute-start | bytes 786440 | tf_op jit(solution)/shard_map/ppermute | solution.py:26
  50.8 8.9 %collective-permute-start.15 = (bf16[1,128,1024]{2,1,0:T(8,128)(2,1)S(1)}, bf16[1,128,1024]{2,1,0:T(8,128)(2,1)S(1)}, u32[]{:S(2)}, u32[]{:S(2)}) collective-permute-start(bf16[1,128,1024]{2,1,0:T(8,128)(2,1)S(1)} %collective-permute-done.14), channel_id=1, source_target_pairs={{1,0},{2,1},{3,2},{4,3},{5,4},{6,5},{7,6},{8,7},{9,8},{10,9},{11,1... | collective-permute-start | bytes 786440 | tf_op jit(solution)/shard_map/ppermute | solution.py:29
  59.0 8.6 %collective-permute-start.9 = (bf16[1,128,1024]{2,1,0:T(8,128)(2,1)S(1)}, bf16[1,128,1024]{2,1,0:T(8,128)(2,1)S(1)}, u32[]{:S(2)}, u32[]{:S(2)}) collective-permute-start(bf16[1,128,1024]{2,1,0:T(8,128)(2,1)S(1)} %collective-permute-done.8), channel_id=1, source_target_pairs={{0,1},{1,2},{2,3},{3,4},{4,5},{5,6},{6,7},{7,8},{8,9},{9,10},{10,1... | collective-permute-start | bytes 786440 | tf_op jit(solution)/shard_map/ppermute | solution.py:26
  59.8 13.8 %collective-permute-start.16 = (bf16[1,128,1024]{2,1,0:T(8,128)(2,1)S(1)}, bf16[1,128,1024]{2,1,0:T(8,128)(2,1)S(1)}, u32[]{:S(2)}, u32[]{:S(2)}) collective-permute-start(bf16[1,128,1024]{2,1,0:T(8,128)(2,1)S(1)} %collective-permute-done.15), channel_id=1, source_target_pairs={{1,0},{2,1},{3,2},{4,3},{5,4},{6,5},{7,6},{8,7},{9,8},{10,9},{11,1... | collective-permute-start | bytes 786440 | tf_op jit(solution)/shard_map/ppermute | solution.py:29
  67.6 11.7 %copy-start.8 = (bf16[1,128,1024]{2,1,0:T(8,128)(2,1)}, bf16[1,128,1024]{2,1,0:T(8,128)(2,1)S(1)}, u32[]{:S(2)}) copy-start(bf16[1,128,1024]{2,1,0:T(8,128)(2,1)S(1)} %collective-permute-done.9) | copy-start | bytes 786436
  67.6 10.8 %collective-permute-start.10 = (bf16[1,128,1024]{2,1,0:T(8,128)(2,1)S(1)}, bf16[1,128,1024]{2,1,0:T(8,128)(2,1)}, u32[]{:S(2)}, u32[]{:S(2)}) collective-permute-start(bf16[1,128,1024]{2,1,0:T(8,128)(2,1)S(1)} %collective-permute-done.9), channel_id=1, source_target_pairs={{0,1},{1,2},{2,3},{3,4},{4,5},{5,6},{6,7},{7,8},{8,9},{9,10},{10,1... | collective-permute-start | bytes 786440 | tf_op jit(solution)/shard_map/ppermute | solution.py:26
  73.5 8.5 %collective-permute-start.17 = (bf16[1,128,1024]{2,1,0:T(8,128)(2,1)S(1)}, bf16[1,128,1024]{2,1,0:T(8,128)(2,1)}, u32[]{:S(2)}, u32[]{:S(2)}) collective-permute-start(bf16[1,128,1024]{2,1,0:T(8,128)(2,1)S(1)} %collective-permute-done.16), channel_id=1, source_target_pairs={{1,0},{2,1},{3,2},{4,3},{5,4},{6,5},{7,6},{8,7},{9,8},{10,9},{11,1... | collective-permute-start | bytes 786440 | tf_op jit(solution)/shard_map/ppermute | solution.py:29
  78.4 8.8 %collective-permute-start.11 = (bf16[1,128,1024]{2,1,0:T(8,128)(2,1)}, bf16[1,128,1024]{2,1,0:T(8,128)(2,1)}, u32[]{:S(2)}, u32[]{:S(2)}) collective-permute-start(bf16[1,128,1024]{2,1,0:T(8,128)(2,1)} %collective-permute-done.10), channel_id=1, source_target_pairs={{0,1},{1,2},{2,3},{3,4},{4,5},{5,6},{6,7},{7,8},{8,9},{9,10},{10,1... | collective-permute-start | bytes 786440 | tf_op jit(solution)/shard_map/ppermute | solution.py:26
  82.0 9.4 %collective-permute-start.18 = (bf16[1,128,1024]{2,1,0:T(8,128)(2,1)}, bf16[1,128,1024]{2,1,0:T(8,128)(2,1)S(1)}, u32[]{:S(2)}, u32[]{:S(2)}) collective-permute-start(bf16[1,128,1024]{2,1,0:T(8,128)(2,1)} %collective-permute-done.17), channel_id=1, source_target_pairs={{1,0},{2,1},{3,2},{4,3},{5,4},{6,5},{7,6},{8,7},{9,8},{10,9},{11,1... | collective-permute-start | bytes 786440 | tf_op jit(solution)/shard_map/ppermute | solution.py:29
  93.4 5.2 %copy-start.3 = (f32[1,2048]{1,0:T(1,128)S(1)}, f32[1,2048]{1,0:T(1,128)}, u32[]{:S(2)}) copy-start(f32[1,2048]{1,0:T(1,128)} %param.22) | copy-start | bytes 24580
  93.4 5.2 %copy-start.10 = (s32[4,1,32]{2,1,0:T(1,128)S(1)}, s32[4,1,32]{2,1,0:T(1,128)}, u32[]{:S(2)}) copy-start(s32[4,1,32]{2,1,0:T(1,128)} %param.17) | copy-start | bytes 1540
  98.6 78.6 %copy-start.5 = (bf16[4,1,32,2048]{3,2,1,0:T(8,128)(2,1)S(1)}, bf16[4,1,32,2048]{3,2,1,0:T(8,128)(2,1)}, u32[]{:S(2)}) copy-start(bf16[4,1,32,2048]{3,2,1,0:T(8,128)(2,1)} %param.23) | copy-start | bytes 1572868
  106.7 5.2 %collective-permute-start = (bf16[1,32,2048]{2,1,0:T(8,128)(2,1)S(1)}, bf16[1,32,2048]{2,1,0:T(8,128)(2,1)S(1)}, u32[]{:S(2)}, u32[]{:S(2)}) collective-permute-start(bf16[1,32,2048]{2,1,0:T(8,128)(2,1)S(1)} %get-tuple-element.1286), channel_id=1, source_target_pairs={{0,16},{1,17},{2,18},{3,19},{4,20},{5,21},{6,22},{7,23},{8,24},{9,... | collective-permute-start | bytes 393224 | tf_op jit(solution)/shard_map/while/body/eval_jaxpr/ppermute | solution.py:42
  108.0 3.8 %collective-permute-start.1 = (bf16[1,32,2048]{2,1,0:T(8,128)(2,1)S(1)}, bf16[1,32,2048]{2,1,0:T(8,128)(2,1)S(1)}, u32[]{:S(2)}, u32[]{:S(2)}) collective-permute-start(bf16[1,32,2048]{2,1,0:T(8,128)(2,1)S(1)} %select_select_fusion.2), channel_id=1, source_target_pairs={{0,16},{1,17},{2,18},{3,19},{4,20},{5,21},{6,22},{7,23},{8,24},{9,... | collective-permute-start | bytes 393224 | tf_op jit(solution)/shard_map/while/body/eval_jaxpr/ppermute | solution.py:42
  119.9 8.3 %collective-permute-start = (bf16[1,32,2048]{2,1,0:T(8,128)(2,1)S(1)}, bf16[1,32,2048]{2,1,0:T(8,128)(2,1)S(1)}, u32[]{:S(2)}, u32[]{:S(2)}) collective-permute-start(bf16[1,32,2048]{2,1,0:T(8,128)(2,1)S(1)} %get-tuple-element.1286), channel_id=1, source_target_pairs={{0,16},{1,17},{2,18},{3,19},{4,20},{5,21},{6,22},{7,23},{8,24},{9,... | collective-permute-start | bytes 393224 | tf_op jit(solution)/shard_map/while/body/eval_jaxpr/ppermute | solution.py:42
  124.3 3.8 %collective-permute-start.1 = (bf16[1,32,2048]{2,1,0:T(8,128)(2,1)S(1)}, bf16[1,32,2048]{2,1,0:T(8,128)(2,1)S(1)}, u32[]{:S(2)}, u32[]{:S(2)}) collective-permute-start(bf16[1,32,2048]{2,1,0:T(8,128)(2,1)S(1)} %select_select_fusion.2), channel_id=1, source_target_pairs={{0,16},{1,17},{2,18},{3,19},{4,20},{5,21},{6,22},{7,23},{8,24},{9,... | collective-permute-start | bytes 393224 | tf_op jit(solution)/shard_map/while/body/eval_jaxpr/ppermute | solution.py:42
  136.2 8.3 %collective-permute-start = (bf16[1,32,2048]{2,1,0:T(8,128)(2,1)S(1)}, bf16[1,32,2048]{2,1,0:T(8,128)(2,1)S(1)}, u32[]{:S(2)}, u32[]{:S(2)}) collective-permute-start(bf16[1,32,2048]{2,1,0:T(8,128)(2,1)S(1)} %get-tuple-element.1286), channel_id=1, source_target_pairs={{0,16},{1,17},{2,18},{3,19},{4,20},{5,21},{6,22},{7,23},{8,24},{9,... | collective-permute-start | bytes 393224 | tf_op jit(solution)/shard_map/while/body/eval_jaxpr/ppermute | solution.py:42
  140.6 3.8 %collective-permute-start.1 = (bf16[1,32,2048]{2,1,0:T(8,128)(2,1)S(1)}, bf16[1,32,2048]{2,1,0:T(8,128)(2,1)S(1)}, u32[]{:S(2)}, u32[]{:S(2)}) collective-permute-start(bf16[1,32,2048]{2,1,0:T(8,128)(2,1)S(1)} %select_select_fusion.2), channel_id=1, source_target_pairs={{0,16},{1,17},{2,18},{3,19},{4,20},{5,21},{6,22},{7,23},{8,24},{9,... | collective-permute-start | bytes 393224 | tf_op jit(solution)/shard_map/while/body/eval_jaxpr/ppermute | solution.py:42
  152.5 8.3 %collective-permute-start = (bf16[1,32,2048]{2,1,0:T(8,128)(2,1)S(1)}, bf16[1,32,2048]{2,1,0:T(8,128)(2,1)S(1)}, u32[]{:S(2)}, u32[]{:S(2)}) collective-permute-start(bf16[1,32,2048]{2,1,0:T(8,128)(2,1)S(1)} %get-tuple-element.1286), channel_id=1, source_target_pairs={{0,16},{1,17},{2,18},{3,19},{4,20},{5,21},{6,22},{7,23},{8,24},{9,... | collective-permute-start | bytes 393224 | tf_op jit(solution)/shard_map/while/body/eval_jaxpr/ppermute | solution.py:42
  156.9 3.8 %collective-permute-start.1 = (bf16[1,32,2048]{2,1,0:T(8,128)(2,1)S(1)}, bf16[1,32,2048]{2,1,0:T(8,128)(2,1)S(1)}, u32[]{:S(2)}, u32[]{:S(2)}) collective-permute-start(bf16[1,32,2048]{2,1,0:T(8,128)(2,1)S(1)} %select_select_fusion.2), channel_id=1, source_target_pairs={{0,16},{1,17},{2,18},{3,19},{4,20},{5,21},{6,22},{7,23},{8,24},{9,... | collective-permute-start | bytes 393224 | tf_op jit(solution)/shard_map/while/body/eval_jaxpr/ppermute | solution.py:42
  161.9 15.2 %collective-permute-start = (bf16[1,32,2048]{2,1,0:T(8,128)(2,1)S(1)}, bf16[1,32,2048]{2,1,0:T(8,128)(2,1)S(1)}, u32[]{:S(2)}, u32[]{:S(2)}) collective-permute-start(bf16[1,32,2048]{2,1,0:T(8,128)(2,1)S(1)} %get-tuple-element.1286), channel_id=1, source_target_pairs={{0,16},{1,17},{2,18},{3,19},{4,20},{5,21},{6,22},{7,23},{8,24},{9,... | collective-permute-start | bytes 393224 | tf_op jit(solution)/shard_map/while/body/eval_jaxpr/ppermute | solution.py:42
  173.2 3.8 %collective-permute-start.1 = (bf16[1,32,2048]{2,1,0:T(8,128)(2,1)S(1)}, bf16[1,32,2048]{2,1,0:T(8,128)(2,1)S(1)}, u32[]{:S(2)}, u32[]{:S(2)}) collective-permute-start(bf16[1,32,2048]{2,1,0:T(8,128)(2,1)S(1)} %select_select_fusion.2), channel_id=1, source_target_pairs={{0,16},{1,17},{2,18},{3,19},{4,20},{5,21},{6,22},{7,23},{8,24},{9,... | collective-permute-start | bytes 393224 | tf_op jit(solution)/shard_map/while/body/eval_jaxpr/ppermute | solution.py:42
  177.3 32.7 %collective-permute-start.2 = (bf16[1,32,2048]{2,1,0:T(8,128)(2,1)S(1)}, bf16[1,32,2048]{2,1,0:T(8,128)(2,1)S(1)}, u32[]{:S(2)}, u32[]{:S(2)}) collective-permute-start(bf16[1,32,2048]{2,1,0:T(8,128)(2,1)S(1)} %get-tuple-element.1160), channel_id=1, source_target_pairs={{16,0},{17,1},{18,2},{19,3},{20,4},{21,5},{22,6},{23,7},{24,8},{25... | collective-permute-start | bytes 393224 | tf_op jit(solution)/shard_map/while/body/eval_jaxpr/ppermute | solution.py:42
  178.6 31.4 %collective-permute-start.3 = (bf16[1,32,2048]{2,1,0:T(8,128)(2,1)S(1)}, bf16[1,32,2048]{2,1,0:T(8,128)(2,1)S(1)}, u32[]{:S(2)}, u32[]{:S(2)}) collective-permute-start(bf16[1,32,2048]{2,1,0:T(8,128)(2,1)S(1)} %get-tuple-element.1161), channel_id=1, source_target_pairs={{16,0},{17,1},{18,2},{19,3},{20,4},{21,5},{22,6},{23,7},{24,8},{25... | collective-permute-start | bytes 393224 | tf_op jit(solution)/shard_map/while/body/eval_jaxpr/ppermute | solution.py:42
  210.1 3.8 %copy-start.2 = (bf16[1024,2048]{1,0:T(8,128)(2,1)S(1)}, bf16[1024,2048]{1,0:T(8,128)(2,1)}, u32[]{:S(2)}) copy-start(bf16[1024,2048]{1,0:T(8,128)(2,1)} %get-tuple-element.750) | copy-start | bytes 12582916 | tf_op jit(solution)/shard_map/while/body/eval_jaxpr/cond
  213.7 2.8 copy-start.1
  218.4 32.7 %collective-permute-start.2 = (bf16[1,32,2048]{2,1,0:T(8,128)(2,1)S(1)}, bf16[1,32,2048]{2,1,0:T(8,128)(2,1)S(1)}, u32[]{:S(2)}, u32[]{:S(2)}) collective-permute-start(bf16[1,32,2048]{2,1,0:T(8,128)(2,1)S(1)} %get-tuple-element.1160), channel_id=1, source_target_pairs={{16,0},{17,1},{18,2},{19,3},{20,4},{21,5},{22,6},{23,7},{24,8},{25... | collective-permute-start | bytes 393224 | tf_op jit(solution)/shard_map/while/body/eval_jaxpr/ppermute | solution.py:42
  219.7 31.4 %collective-permute-start.3 = (bf16[1,32,2048]{2,1,0:T(8,128)(2,1)S(1)}, bf16[1,32,2048]{2,1,0:T(8,128)(2,1)S(1)}, u32[]{:S(2)}, u32[]{:S(2)}) collective-permute-start(bf16[1,32,2048]{2,1,0:T(8,128)(2,1)S(1)} %get-tuple-element.1161), channel_id=1, source_target_pairs={{16,0},{17,1},{18,2},{19,3},{20,4},{21,5},{22,6},{23,7},{24,8},{25... | collective-permute-start | bytes 393224 | tf_op jit(solution)/shard_map/while/body/eval_jaxpr/ppermute | solution.py:42
  251.2 3.8 %copy-start.2 = (bf16[1024,2048]{1,0:T(8,128)(2,1)S(1)}, bf16[1024,2048]{1,0:T(8,128)(2,1)}, u32[]{:S(2)}) copy-start(bf16[1024,2048]{1,0:T(8,128)(2,1)} %get-tuple-element.750) | copy-start | bytes 12582916 | tf_op jit(solution)/shard_map/while/body/eval_jaxpr/cond
  254.8 2.8 copy-start.1
  259.5 32.7 %collective-permute-start.2 = (bf16[1,32,2048]{2,1,0:T(8,128)(2,1)S(1)}, bf16[1,32,2048]{2,1,0:T(8,128)(2,1)S(1)}, u32[]{:S(2)}, u32[]{:S(2)}) collective-permute-start(bf16[1,32,2048]{2,1,0:T(8,128)(2,1)S(1)} %get-tuple-element.1160), channel_id=1, source_target_pairs={{16,0},{17,1},{18,2},{19,3},{20,4},{21,5},{22,6},{23,7},{24,8},{25... | collective-permute-start | bytes 393224 | tf_op jit(solution)/shard_map/while/body/eval_jaxpr/ppermute | solution.py:42
  260.8 31.4 %collective-permute-start.3 = (bf16[1,32,2048]{2,1,0:T(8,128)(2,1)S(1)}, bf16[1,32,2048]{2,1,0:T(8,128)(2,1)S(1)}, u32[]{:S(2)}, u32[]{:S(2)}) collective-permute-start(bf16[1,32,2048]{2,1,0:T(8,128)(2,1)S(1)} %get-tuple-element.1161), channel_id=1, source_target_pairs={{16,0},{17,1},{18,2},{19,3},{20,4},{21,5},{22,6},{23,7},{24,8},{25... | collective-permute-start | bytes 393224 | tf_op jit(solution)/shard_map/while/body/eval_jaxpr/ppermute | solution.py:42
  292.3 3.8 %copy-start.2 = (bf16[1024,2048]{1,0:T(8,128)(2,1)S(1)}, bf16[1024,2048]{1,0:T(8,128)(2,1)}, u32[]{:S(2)}) copy-start(bf16[1024,2048]{1,0:T(8,128)(2,1)} %get-tuple-element.750) | copy-start | bytes 12582916 | tf_op jit(solution)/shard_map/while/body/eval_jaxpr/cond
  300.5 32.7 %collective-permute-start.2 = (bf16[1,32,2048]{2,1,0:T(8,128)(2,1)S(1)}, bf16[1,32,2048]{2,1,0:T(8,128)(2,1)S(1)}, u32[]{:S(2)}, u32[]{:S(2)}) collective-permute-start(bf16[1,32,2048]{2,1,0:T(8,128)(2,1)S(1)} %get-tuple-element.1160), channel_id=1, source_target_pairs={{16,0},{17,1},{18,2},{19,3},{20,4},{21,5},{22,6},{23,7},{24,8},{25... | collective-permute-start | bytes 393224 | tf_op jit(solution)/shard_map/while/body/eval_jaxpr/ppermute | solution.py:42
  301.8 31.4 %collective-permute-start.3 = (bf16[1,32,2048]{2,1,0:T(8,128)(2,1)S(1)}, bf16[1,32,2048]{2,1,0:T(8,128)(2,1)S(1)}, u32[]{:S(2)}, u32[]{:S(2)}) collective-permute-start(bf16[1,32,2048]{2,1,0:T(8,128)(2,1)S(1)} %get-tuple-element.1161), channel_id=1, source_target_pairs={{16,0},{17,1},{18,2},{19,3},{20,4},{21,5},{22,6},{23,7},{24,8},{25... | collective-permute-start | bytes 393224 | tf_op jit(solution)/shard_map/while/body/eval_jaxpr/ppermute | solution.py:42
  333.3 3.8 %copy-start.2 = (bf16[1024,2048]{1,0:T(8,128)(2,1)S(1)}, bf16[1024,2048]{1,0:T(8,128)(2,1)}, u32[]{:S(2)}) copy-start(bf16[1024,2048]{1,0:T(8,128)(2,1)} %get-tuple-element.750) | copy-start | bytes 12582916 | tf_op jit(solution)/shard_map/while/body/eval_jaxpr/cond
  341.6 32.7 %collective-permute-start.2 = (bf16[1,32,2048]{2,1,0:T(8,128)(2,1)S(1)}, bf16[1,32,2048]{2,1,0:T(8,128)(2,1)S(1)}, u32[]{:S(2)}, u32[]{:S(2)}) collective-permute-start(bf16[1,32,2048]{2,1,0:T(8,128)(2,1)S(1)} %get-tuple-element.1160), channel_id=1, source_target_pairs={{16,0},{17,1},{18,2},{19,3},{20,4},{21,5},{22,6},{23,7},{24,8},{25... | collective-permute-start | bytes 393224 | tf_op jit(solution)/shard_map/while/body/eval_jaxpr/ppermute | solution.py:42
  342.9 31.4 %collective-permute-start.3 = (bf16[1,32,2048]{2,1,0:T(8,128)(2,1)S(1)}, bf16[1,32,2048]{2,1,0:T(8,128)(2,1)S(1)}, u32[]{:S(2)}, u32[]{:S(2)}) collective-permute-start(bf16[1,32,2048]{2,1,0:T(8,128)(2,1)S(1)} %get-tuple-element.1161), channel_id=1, source_target_pairs={{16,0},{17,1},{18,2},{19,3},{20,4},{21,5},{22,6},{23,7},{24,8},{25... | collective-permute-start | bytes 393224 | tf_op jit(solution)/shard_map/while/body/eval_jaxpr/ppermute | solution.py:42
  (5 other events, 9.1 us)
Sparse Core Ops, SparseCore 0:
  10.2 68.1 all-gather.1
